TPU v7x, 32 devices: a whole 2x2x4 slice. The times are simulated.
32 devices in a mesh: dp: 16 (over z, y, core), tensor: 2 (over x).
Axes of the slice: x: 2, y: 2, z: 4, core: 2. Of those that a mesh axis runs over, the one named last changes fastest.
Arguments:
- hidden_states: bfloat16 [8192, 2048], P('dp', 'tensor'), may hold values from -6 to 6
- norm_gain: bfloat16 [2048], replicated, may hold values from 0.25 to 1.75
- head_weight: bfloat16 [2048, 25600], P(None, ('tensor', 'dp')), may hold values from -1 to 1
- target_ids: int32 [8192], P('dp'), may hold values from 0 to 25599
- loss_mask: int32 [8192], P('dp'), may hold values from 0 to 1, as said below
- seq_lengths: int32 [16], replicated, may hold values from 1 to 4096, as said below
- slot_order: int32 [16], replicated, may hold values from 0 to 15, each once
Outputs:
- token_logprob: float32 [8192], P(('dp', 'tensor'))
- token_entropy: float32 [8192], P(('dp', 'tensor'))
- seq_mean_logprob: float32 [16], P('dp')
- seq_mean_entropy: float32 [16], P('dp')
Inputs may be any that keep to these rules, and one draw needn't show every extreme that they name: `seq_lengths`: sequences lie in packed order, one after another; their lengths sum to 8192; the longest has exactly 4096 tokens and some sequence has exactly 1 token. `slot_order`: each sequence appears once. `loss_mask`: some sequence of exactly 1 token has no scored row.
All inputs are finite; a program needn't handle non-finite values.
Results may differ from a plain program's by a relative error of at most 0.0012.
Values may be sent and summed in bfloat16 or wider, within the bound.
No kernel may reach another device: no remote copies, remote signals or barrier semaphores. Data moves between devices by JAX's collectives and lax.ppermute only.
A program may use at most 192 MiB of HBM per device.

v0:
```python
import jax
import jax.numpy as jnp
from jax import lax
from jax.sharding import PartitionSpec as P

EPS = 1e-05


def per_device(
    hidden_states, norm_gain, head_weight, target_ids, loss_mask, seq_lengths, slot_order
):
    whole = lax.all_gather(hidden_states, "tensor", axis=1, tiled=True)
    values = whole.astype(jnp.float32)
    square = jnp.mean(values * values, axis=1, keepdims=True)
    normed = (values * lax.rsqrt(square + EPS) * norm_gain.astype(jnp.float32)).astype(jnp.bfloat16)
    rows = whole.shape[0]
    groups = lax.axis_size("tensor")
    share = rows // groups
    column_base = lax.axis_index("tensor") * (head_weight.shape[1] * lax.axis_size("dp"))
    piece = lax.all_gather(head_weight, "dp", axis=1, tiled=True)
    top = jnp.full((rows,), -1e30, jnp.float32)
    total = jnp.zeros((rows,), jnp.float32)
    logits = jnp.dot(normed, piece, preferred_element_type=jnp.float32)
    columns = column_base + lax.broadcasted_iota(jnp.int32, (1, piece.shape[1]), 1)
    new_top = jnp.maximum(top, jnp.max(logits, axis=1))
    shifted = logits - new_top[:, None]
    expo = jnp.exp(shifted)
    scale = jnp.exp(top - new_top)
    new_total = jnp.sum(expo, axis=1)
    new_spread = scale * (total * (top - new_top)) + jnp.sum(expo * shifted, axis=1)
    hit = jnp.sum(jnp.where(columns == target_ids[:, None], logits, 0.0), axis=1)
    mine = lax.axis_index("tensor") * share
    row_top = lax.pmax(new_top, "tensor")
    scale = jnp.exp(new_top - row_top)
    sums = lax.psum(
        (new_total * scale, scale * (new_spread + new_total * (new_top - row_top)), hit), "tensor"
    )
    row_top = lax.dynamic_slice_in_dim(row_top, mine, share)
    row_total = lax.dynamic_slice_in_dim(sums[0], mine, share)
    row_spread = lax.dynamic_slice_in_dim(sums[1], mine, share)
    row_picked = lax.dynamic_slice_in_dim(sums[2], mine, share)
    logsum = jnp.log(row_total)
    live = lax.dynamic_slice_in_dim(loss_mask, mine, share).astype(jnp.float32)
    token_logprob = (row_picked - row_top - logsum) * live
    token_entropy = (logsum - row_spread / row_total) * live
    ends = jnp.cumsum(seq_lengths)
    position = lax.axis_index("dp") * rows + mine + jnp.arange(share, dtype=jnp.int32)
    segment = jnp.sum((position[:, None] >= ends[None, :]).astype(jnp.int32), axis=1)
    member = (segment[:, None] == slot_order[None, :]).astype(jnp.float32)
    lp_part = jnp.dot(token_logprob, member, precision=lax.Precision.HIGHEST)
    ent_part = jnp.dot(token_entropy, member, precision=lax.Precision.HIGHEST)
    count_part = jnp.dot(live, member, precision=lax.Precision.HIGHEST)
    lp_sum, ent_sum, count = lax.psum((lp_part, ent_part, count_part), ("dp", "tensor"))
    owned = lp_sum.shape[0] // lax.axis_size("dp")
    first_slot = lax.axis_index("dp") * owned
    floor = jnp.maximum(lax.dynamic_slice_in_dim(count, first_slot, owned), 1.0)
    seq_mean_logprob = lax.dynamic_slice_in_dim(lp_sum, first_slot, owned) / floor
    seq_mean_entropy = lax.dynamic_slice_in_dim(ent_sum, first_slot, owned) / floor
    return (token_logprob, token_entropy, seq_mean_logprob, seq_mean_entropy)


def solution(mesh):
    placed = (P("dp", "tensor"), P(), P(None, ("tensor", "dp")), P("dp"), P("dp"), P(), P())
    return jax.shard_map(
        per_device,
        mesh=mesh,
        in_specs=placed,
        out_specs=(P(("dp", "tensor")), P(("dp", "tensor")), P("dp"), P("dp")),
        check_vma=False,
    )
```

profile of v0, /device:TPU:0, one launch (start us, length us, event | category | flops | bytes accessed | tf_op | source)
XLA Modules:
  0.0 416.9 jit_solution(15467861116896965682)
XLA Ops:
  7.2 0.0 all-gather.3.cloned.1.call-start
  7.2 0.7 all-gather.3.cloned.1.call-update
  7.9 0.0 all-gather.5.cloned.1.call-start
  7.9 0.7 all-gather.5.cloned.1.call-update
  8.7 0.7 convert_element_type.17
  9.3 0.7 copy.13
  10.1 0.1 reduce
  10.2 0.1 convert_reduce_fusion
  10.3 35.1 %all-gather.3.cloned.1.call-done = bf16[512,2048]{1,0:T(8,128)(2,1)} async-done(((bf16[512,1024]{1,0:T(8,128)(2,1)}), bf16[512,2048]{1,0:T(8,128)(2,1)}) %all-gather.3.cloned.1.call-update) | async-done | bytes 2097168 | tf_op jit(solution)/shard_map/all_gather | solution.py:12
  45.4 2.1 fusion.1
  47.5 0.0 copy-start
  47.5 256.5 %all-gather.5.cloned.1.call-done = bf16[2048,12800]{0,1:T(8,128)(2,1)} async-done(((bf16[2048,800]{0,1:T(8,128)(2,1)}), bf16[2048,12800]{0,1:T(8,128)(2,1)}) %all-gather.5.cloned.1.call-update) | async-done | bytes 52428816 | tf_op jit(solution)/shard_map/all_gather | solution.py:20
  304.0 35.8 %fusion.17 = (f32[512]{0:T(512)S(1)}, f32[512,12800]{1,0:T(8,128)}) fusion(bf16[2048,12800]{0,1:T(8,128)(2,1)} %all-gather.5.cloned.1.call-done, bf16[512,2048]{1,0:T(8,128)(2,1)} %all-gather.3.cloned.1.call-done, f32[2048]{0:T(1024)S(1)} %convert_element_type.17, f32[512]{0:T(512)S(1)} %add_rsqrt_fusion), kind=kOutput, calls=%fused_computation.34 | convolution fusion | flops 26854293504 | bytes 80752640 | tf_op jit(solution)/shard_map/dot_general | solution.py:23
  339.9 0.0 copy-start.3
  339.9 0.0 copy-start.4
  339.9 4.9 %pmax.7 = f32[512]{0:T(512)S(1)} all-reduce(f32[512]{0:T(512)S(1)} %broadcast_maximum_fusion), channel_id=1, replica_groups=mesh['dp'=16,'tensor'=2] {'tensor'}, use_global_device_ids=true, to_apply=%region_4.5 | all-reduce | flops 512 | bytes 4096 | tf_op jit(solution)/shard_map/pmax | solution.py:33
  344.8 0.0 copy-done
  344.8 13.5 %fusion = (f32[512]{0:T(512)S(1)}, f32[512]{0:T(512)S(1)}, f32[512]{0:T(512)S(1)}) fusion(f32[512,12800]{1,0:T(8,128)} %get-tuple-element.18, f32[512]{0:T(512)S(1)} %broadcast_maximum_fusion, s32[512]{0:T(512)S(1)} %copy-done, s32[12800]{0:T(1024)S(1)} %iota_add_fusion), kind=kLoop, calls=%fused_computation.2 | loop fusion | flops 45873664 | bytes 26275840 | tf_op jit(solution)/shard_map/reduce_sum | solution.py:30
  358.3 5.0 %all-reduce.1 = (f32[512]{0:T(512)S(1)}, f32[512]{0:T(512)S(1)}, f32[512]{0:T(512)S(1)}) all-reduce(f32[512]{0:T(512)S(1)} %get-tuple-element.6, f32[512]{0:T(512)S(1)} %get-tuple-element.16, f32[512]{0:T(512)S(1)} %get-tuple-element.15), channel_id=1, replica_groups=mesh['dp'=16,'tensor'=2] {'tensor'}, use_global_device_ids=true, to_apply=%region_2.0 | all-reduce | flops 1536 | bytes 12288 | tf_op jit(solution)/shard_map/psum | solution.py:35
  363.3 0.0 copy-done.3
  363.3 0.1 subtract_multiply_fusion
  363.4 0.0 copy-start.1
  363.4 0.0 copy-done.4
  363.4 0.2 convolution_bitcast_fusion
  363.6 0.2 convolution_bitcast_fusion.1
  363.9 0.1 subtract_multiply_fusion.1
  364.0 0.0 copy-start.2
  364.0 0.2 convolution_bitcast_fusion.2
  364.2 39.7 %all-reduce = (f32[16]{0:T(128)S(1)}, f32[16]{0:T(128)S(1)}, f32[16]{0:T(128)S(1)}) all-reduce(f32[16]{0:T(128)S(1)} %convolution_bitcast_fusion.2, f32[16]{0:T(128)S(1)} %convolution_bitcast_fusion.1, f32[16]{0:T(128)S(1)} %convolution_bitcast_fusion), channel_id=1, replica_groups=mesh['dp'=16,'tensor'=2] {'dp','tensor'}, use_global_device_ids=true, to_apply=%region_11.12 | all-reduce | flops 48 | bytes 384 | tf_op jit(solution)/shard_map/psum | solution.py:53
  403.9 0.7 dynamic_slice.31
  404.6 0.6 dynamic_slice.30
  405.2 0.6 dynamic_slice.29
  407.8 0.0 copy-done.1
  407.8 0.0 copy-done.2
  (6 shorter events, 0.1 us)
Async XLA Ops:
  7.2 38.3 %all-gather.3.cloned.1.call-start = ((), (), s32[]{:S(2)}) async-start(), calls=%async_computation | async-start | bytes 3145728 | tf_op jit(solution)/shard_map/all_gather | solution.py:12
  7.9 296.1 %all-gather.5.cloned.1.call-start = ((), (), s32[]{:S(2)}) async-start(), calls=%async_computation.1 | async-start | bytes 55705600 | tf_op jit(solution)/shard_map/all_gather | solution.py:20
  47.5 297.3 %copy-start = (s32[512]{0:T(512)S(1)}, s32[512]{0:T(512)}, u32[]{:S(2)}) copy-start(s32[512]{0:T(512)} %param.10) | copy-start | bytes 6148
  339.9 23.5 %copy-start.3 = (s32[512]{0:T(512)S(1)}, s32[512]{0:T(512)}, u32[]{:S(2)}) copy-start(s32[512]{0:T(512)} %param.11) | copy-start | bytes 6148
  339.9 23.6 %copy-start.4 = (s32[16]{0:T(128)S(1)}, s32[16]{0:T(128)}, u32[]{:S(2)}) copy-start(s32[16]{0:T(128)} %param.13) | copy-start | bytes 196
  363.4 44.3 %copy-start.1 = (f32[256]{0:T(256)}, f32[256]{0:T(256)S(1)}, u32[]{:S(2)}) copy-start(f32[256]{0:T(256)S(1)} %get-tuple-element.13) | copy-start | bytes 3076
  364.0 43.8 %copy-start.2 = (f32[256]{0:T(256)}, f32[256]{0:T(256)S(1)}, u32[]{:S(2)}) copy-start(f32[256]{0:T(256)S(1)} %subtract_multiply_fusion.1) | copy-start | bytes 3076
Sparse Core Ops, SparseCore 0:
  9.5 35.8 all-gather.2
  47.0 256.9 all-gather.4
where the time goes:
time: 417 us
  waiting for transfers between devices  293 us (70%)
  blocking collectives  49.7 us (12%)
  matrix products  36.5 us (9%)
  between operations  18.3 us (4%)
  other arithmetic  16.7 us (4%)
    all_gather x1, waiting for transfers between devices, per_device(): piece = lax.all_gather(head_weight, 'dp', axis=1, tiled=True)  257 us
    psum x1, blocking collectives, per_device(): lax.psum((lp_part, ent_part, count_part), ('dp', 'tensor'))  39.7 us
    dot_general x1, matrix products, per_device(): logits = jnp.dot(normed, piece, preferred_element_type=jnp.float32)  35.8 us
    all_gather x1, waiting for transfers between devices, per_device(): whole = lax.all_gather(hidden_states, 'tensor', axis=1, tiled=True)  35.1 us
    reduce_sum x1, other arithmetic, per_device(): jnp.sum(expo * shifted, axis=1)  13.5 us
  transfers between devices with their start and end apart: 2, of which 2 were waited for; matrix products, arithmetic and copies ran while one was open for 1% of the time, Pallas kernels for 0%

commit v1 on v0

--- a/solution.py
+++ b/solution.py
@@ -17,7 +17,21 @@
     groups = lax.axis_size("tensor")
     share = rows // groups
     column_base = lax.axis_index("tensor") * (head_weight.shape[1] * lax.axis_size("dp"))
-    piece = lax.all_gather(head_weight, "dp", axis=1, tiled=True)
+    ways, here, step = (lax.axis_size("dp"), lax.axis_index("dp"), head_weight.shape[1])
+    shape = [n * ways if d == 1 else n for d, n in enumerate(head_weight.shape)]
+    full = lax.dynamic_update_slice_in_dim(
+        jnp.zeros(shape, head_weight.dtype), head_weight, here * step, axis=1
+    )
+    going_up = going_down = head_weight
+    for far in range(1, ways // 2 + 1):
+        going_up = lax.ppermute(going_up, "dp", [(d, (d + 1) % ways) for d in range(ways)])
+        full = lax.dynamic_update_slice_in_dim(full, going_up, (here - far) % ways * step, axis=1)
+        if 2 * far < ways:
+            going_down = lax.ppermute(going_down, "dp", [(d, (d - 1) % ways) for d in range(ways)])
+            full = lax.dynamic_update_slice_in_dim(
+                full, going_down, (here + far) % ways * step, axis=1
+            )
+    piece = full
     top = jnp.full((rows,), -1e30, jnp.float32)
     total = jnp.zeros((rows,), jnp.float32)
     logits = jnp.dot(normed, piece, preferred_element_type=jnp.float32)

time: 417 us -> 671 us (1.61)
  starting transfers between devices: 0.08 us -> 405 us
  waiting for transfers between devices: 293 us -> 67.7 us
  local copies, waits for them, and re-layouts: 2.58 us -> 68.5 us
  blocking collectives: 49.7 us -> 57.7 us
    ppermute x0 -> x15, starting transfers between devices: none -> 405 us  [the longest x8 400 us: per_device(): lax.ppermute(going_up, 'dp', [(d, (d + 1) % ways) for d in range(ways)])]
    all_gather x1 -> x0, waiting for transfers between devices: 257 us -> none  [per_device(): piece = lax.all_gather(head_weight, 'dp', axis=1, tiled=True)]
    ppermute x0 -> x15, waiting for transfers between devices: none -> 67.7 us  [the longest x8 67.7 us: per_device(): lax.ppermute(going_up, 'dp', [(d, (d + 1) % ways) for d in range(ways)])]
    dynamic_update_slice x0 -> x16, local copies, waits for them, and re-layouts: none -> 48.9 us  [the longest x8 26.7 us: per_device(): lax.dynamic_update_slice_in_dim(full, going_up, (here - far) % ways * ste...]
    all_gather x1, waiting for transfers between devices: 35.1 us -> 0.01 us  [per_device(): whole = lax.all_gather(hidden_states, 'tensor', axis=1, tiled=True)]
    broadcast_in_dim x0 -> x1, local copies, waits for them, and re-layouts: none -> 17 us  [per_device(): jnp.zeros(shape, head_weight.dtype)]
    psum x1, blocking collectives: 39.7 us -> 47.6 us  [per_device(): lax.psum((lp_part, ent_part, count_part), ('dp', 'tensor'))]
  transfers between devices with their start and end apart: 2 -> 16, of which waited for: 2 -> 6; matrix products, arithmetic and copies ran while one was open for 1% -> 10% of each run, Pallas kernels for 0% -> 0%
where the time goes in v1:
time: 671 us; the launch traced here: 670 us
  starting transfers between devices  405 us (60%)
  local copies, waits for them, and re-layouts  68.5 us (10%)
  waiting for transfers between devices  67.7 us (10%)
  blocking collectives  57.7 us (9%)
  matrix products  35.7 us (5%)
  between operations  18.4 us (3%)
  other arithmetic  16.9 us (3%)
    ppermute x8, starting transfers between devices, per_device(): lax.ppermute(going_up, 'dp', [(d, (d + 1) % ways) for d in range(ways)])  400 us
    ppermute x8, waiting for transfers between devices, per_device(): lax.ppermute(going_up, 'dp', [(d, (d + 1) % ways) for d in range(ways)])  67.7 us
    psum x1, blocking collectives, per_device(): lax.psum((lp_part, ent_part, count_part), ('dp', 'tensor'))  47.6 us
    dot_general x1, matrix products, per_device(): logits = jnp.dot(normed, piece, preferred_element_type=jnp.float32)  35 us
    dynamic_update_slice x8, local copies, waits for them, and re-layouts, per_device(): lax.dynamic_update_slice_in_dim(full, going_up, (here - far) % ways * ste...  26.7 us
    dynamic_update_slice x7, local copies, waits for them, and re-layouts, per_device(): lax.dynamic_update_slice_in_dim(full, going_down, (here + far) % ways * s...  20.3 us
    broadcast_in_dim x1, local copies, waits for them, and re-layouts, per_device(): jnp.zeros(shape, head_weight.dtype)  17 us
    reduce_sum x1, other arithmetic, per_device(): jnp.sum(expo * shifted, axis=1)  13.5 us
  transfers between devices with their start and end apart: 16, of which 6 were waited for; matrix products, arithmetic and copies ran while one was open for 10% of the time, Pallas kernels for 0%

profile of v1, /device:TPU:0, one launch (start us, length us, event | category | flops | bytes accessed | tf_op | source)
XLA Modules:
  0.0 670.2 jit_solution(15362073734753085879)
XLA Ops:
  7.2 0.5 collective-permute-start
  7.7 5.1 collective-permute-start.1
  12.8 36.6 %collective-permute-done = bf16[2048,800]{0,1:T(8,128)(2,1)S(1)} collective-permute-done((bf16[2048,800]{0,1:T(8,128)(2,1)}, bf16[2048,800]{0,1:T(8,128)(2,1)S(1)}, u32[]{:S(2)}, u32[]{:S(2)}) %collective-permute-start) | collective-permute-done | bytes 3276832 | tf_op jit(solution)/shard_map/ppermute | solution.py:27
  49.4 32.0 %collective-permute-start.2 = (bf16[2048,800]{0,1:T(8,128)(2,1)S(1)}, bf16[2048,800]{0,1:T(8,128)(2,1)S(1)}, u32[]{:S(2)}, u32[]{:S(2)}) collective-permute-start(bf16[2048,800]{0,1:T(8,128)(2,1)S(1)} %collective-permute-done), channel_id=1, source_target_pairs={{0,2},{2,4},{4,6},{6,8},{8,10},{10,12},{12,14},{14,16},{16,18},{18... | collective-permute-start | bytes 9830408 | tf_op jit(solution)/shard_map/ppermute | solution.py:27
  81.4 8.9 %collective-permute-done.2 = bf16[2048,800]{0,1:T(8,128)(2,1)S(1)} collective-permute-done((bf16[2048,800]{0,1:T(8,128)(2,1)S(1)}, bf16[2048,800]{0,1:T(8,128)(2,1)S(1)}, u32[]{:S(2)}, u32[]{:S(2)}) %collective-permute-start.2) | collective-permute-done | bytes 3276832 | tf_op jit(solution)/shard_map/ppermute | solution.py:27
  90.3 63.5 %collective-permute-start.4 = (bf16[2048,800]{0,1:T(8,128)(2,1)S(1)}, bf16[2048,800]{0,1:T(8,128)(2,1)S(1)}, u32[]{:S(2)}, u32[]{:S(2)}) collective-permute-start(bf16[2048,800]{0,1:T(8,128)(2,1)S(1)} %collective-permute-done.2), channel_id=1, source_target_pairs={{0,2},{2,4},{4,6},{6,8},{8,10},{10,12},{12,14},{14,16},{16,18},{18... | collective-permute-start | bytes 9830408 | tf_op jit(solution)/shard_map/ppermute | solution.py:27
  153.8 5.5 collective-permute-done.4
  159.3 67.0 %collective-permute-start.6 = (bf16[2048,800]{0,1:T(8,128)(2,1)S(1)}, bf16[2048,800]{0,1:T(8,128)(2,1)S(1)}, u32[]{:S(2)}, u32[]{:S(2)}) collective-permute-start(bf16[2048,800]{0,1:T(8,128)(2,1)S(1)} %collective-permute-done.4), channel_id=1, source_target_pairs={{0,2},{2,4},{4,6},{6,8},{8,10},{10,12},{12,14},{14,16},{16,18},{18... | collective-permute-start | bytes 9830408 | tf_op jit(solution)/shard_map/ppermute | solution.py:27
  226.4 5.4 collective-permute-done.6
  231.8 67.0 %collective-permute-start.8 = (bf16[2048,800]{0,1:T(8,128)(2,1)S(1)}, bf16[2048,800]{0,1:T(8,128)(2,1)}, u32[]{:S(2)}, u32[]{:S(2)}) collective-permute-start(bf16[2048,800]{0,1:T(8,128)(2,1)S(1)} %collective-permute-done.6), channel_id=1, source_target_pairs={{0,2},{2,4},{4,6},{6,8},{8,10},{10,12},{12,14},{14,16},{16,18},{18... | collective-permute-start | bytes 9830408 | tf_op jit(solution)/shard_map/ppermute | solution.py:27
  298.9 5.5 collective-permute-done.8
  304.4 65.6 %collective-permute-start.10 = (bf16[2048,800]{0,1:T(8,128)(2,1)}, bf16[2048,800]{0,1:T(8,128)(2,1)}, u32[]{:S(2)}, u32[]{:S(2)}) collective-permute-start(bf16[2048,800]{0,1:T(8,128)(2,1)} %collective-permute-done.8), channel_id=1, source_target_pairs={{0,2},{2,4},{4,6},{6,8},{8,10},{10,12},{12,14},{14,16},{16,18},{18... | collective-permute-start | bytes 9830408 | tf_op jit(solution)/shard_map/ppermute | solution.py:27
  370.0 5.8 collective-permute-done.10
  375.8 66.9 %collective-permute-start.12 = (bf16[2048,800]{0,1:T(8,128)(2,1)}, bf16[2048,800]{0,1:T(8,128)(2,1)}, u32[]{:S(2)}, u32[]{:S(2)}) collective-permute-start(bf16[2048,800]{0,1:T(8,128)(2,1)} %collective-permute-done.10), channel_id=1, source_target_pairs={{0,2},{2,4},{4,6},{6,8},{8,10},{10,12},{12,14},{14,16},{16,18},{18... | collective-permute-start | bytes 9830408 | tf_op jit(solution)/shard_map/ppermute | solution.py:27
  442.7 0.7 convert_element_type.17
  443.4 0.7 copy.13
  444.2 0.1 reduce
  444.5 17.0 %broadcast_in_dim.10 = bf16[2048,12800]{0,1:T(8,128)(2,1)} broadcast(bf16[]{:T(256)} %constant.110.clone.1), dimensions={} | broadcast | bytes 52428800 | tf_op jit(solution)/shard_map/broadcast_in_dim | solution.py:23
  461.5 1.9 constant_dynamic-update-slice_fusion.15
  463.4 2.2 fusion.1
  465.7 4.8 constant_dynamic-update-slice_fusion.14
  470.5 4.1 constant_dynamic-update-slice_fusion.13
  474.6 4.0 constant_dynamic-update-slice_fusion.12
  478.6 37.6 %collective-permute-start.14 = (bf16[2048,800]{0,1:T(8,128)(2,1)}, bf16[2048,800]{0,1:T(8,128)(2,1)S(1)}, u32[]{:S(2)}, u32[]{:S(2)}) collective-permute-start(bf16[2048,800]{0,1:T(8,128)(2,1)} %collective-permute-done.12), channel_id=1, source_target_pairs={{0,2},{2,4},{4,6},{6,8},{8,10},{10,12},{12,14},{14,16},{16,18},{18... | collective-permute-start | bytes 9830408 | tf_op jit(solution)/shard_map/ppermute | solution.py:27
  516.2 2.2 constant_dynamic-update-slice_fusion.11
  518.4 1.9 constant_dynamic-update-slice_fusion.10
  520.3 2.0 constant_dynamic-update-slice_fusion.9
  522.3 2.0 constant_dynamic-update-slice_fusion.8
  524.2 1.9 constant_dynamic-update-slice_fusion.7
  526.1 4.0 constant_dynamic-update-slice_fusion.6
  530.2 4.1 constant_dynamic-update-slice_fusion.5
  534.2 4.0 constant_dynamic-update-slice_fusion.4
  538.2 4.1 constant_dynamic-update-slice_fusion.3
  542.3 4.0 constant_dynamic-update-slice_fusion.2
  546.4 2.0 constant_dynamic-update-slice_fusion.1
  548.4 1.9 constant_dynamic-update-slice_fusion
  550.3 35.0 %fusion.17 = (f32[512]{0:T(512)S(1)}, f32[512,12800]{1,0:T(8,128)}) fusion(bf16[2048,12800]{0,1:T(8,128)(2,1)} %constant_dynamic-update-slice_fusion, bf16[512,2048]{1,0:T(8,128)(2,1)S(1)} %copy-done.12, f32[2048]{0:T(1024)S(1)} %convert_element_type.17, f32[512]{0:T(512)S(1)} %add_rsqrt_fusion), kind=kOutput, calls=%fused_computation.50 | convolution fusion | flops 26854293504 | bytes 80752640 | tf_op jit(solution)/shard_map/dot_general | solution.py:37
  585.3 5.1 pmax.7
  590.4 13.5 %fusion = (f32[512]{0:T(512)S(1)}, f32[512]{0:T(512)S(1)}, f32[512]{0:T(512)S(1)}) fusion(f32[512,12800]{1,0:T(8,128)} %get-tuple-element.18, f32[512]{0:T(512)S(1)} %broadcast_maximum_fusion, s32[512]{0:T(512)S(1)} %copy-done.13, s32[12800]{0:T(1024)S(1)} %iota_add_fusion), kind=kLoop, calls=%fused_computation.2 | loop fusion | flops 45873664 | bytes 26275840 | tf_op jit(solution)/shard_map/reduce_sum | solution.py:44
  603.9 5.0 all-reduce.1
  609.0 0.2 convolution_bitcast_fusion
  609.2 0.2 convolution_bitcast_fusion.1
  609.5 0.1 subtract_multiply_fusion.1
  609.6 0.2 convolution_bitcast_fusion.2
  609.8 47.6 %all-reduce = (f32[16]{0:T(128)S(1)}, f32[16]{0:T(128)S(1)}, f32[16]{0:T(128)S(1)}) all-reduce(f32[16]{0:T(128)S(1)} %convolution_bitcast_fusion.2, f32[16]{0:T(128)S(1)} %convolution_bitcast_fusion.1, f32[16]{0:T(128)S(1)} %convolution_bitcast_fusion), channel_id=1, replica_groups=mesh['dp'=16,'tensor'=2] {'dp','tensor'}, use_global_device_ids=true, to_apply=%region_11.12 | all-reduce | flops 48 | bytes 384 | tf_op jit(solution)/shard_map/psum | solution.py:67
  657.4 0.6 dynamic_slice.31
  658.0 0.6 dynamic_slice.30
  658.6 0.6 dynamic_slice.29
  (62 shorter events, 0.5 us)
Async XLA Ops:
  7.2 456.3 %all-gather.2.cloned.1.call-start = ((), (), s32[]{:S(2)}) async-start(), calls=%async_computation | async-start | bytes 3145728 | tf_op jit(solution)/shard_map/all_gather | solution.py:12
  7.2 42.2 %collective-permute-start = (bf16[2048,800]{0,1:T(8,128)(2,1)}, bf16[2048,800]{0,1:T(8,128)(2,1)S(1)}, u32[]{:S(2)}, u32[]{:S(2)}) collective-permute-start(bf16[2048,800]{0,1:T(8,128)(2,1)} %param.9), channel_id=1, source_target_pairs={{0,2},{2,4},{4,6},{6,8},{8,10},{10,12},{12,14},{14,16},{16,18},{18... | collective-permute-start | bytes 9830408 | tf_op jit(solution)/shard_map/ppermute | solution.py:27
  7.7 73.7 %collective-permute-start.1 = (bf16[2048,800]{0,1:T(8,128)(2,1)}, bf16[2048,800]{0,1:T(8,128)(2,1)S(1)}, u32[]{:S(2)}, u32[]{:S(2)}) collective-permute-start(bf16[2048,800]{0,1:T(8,128)(2,1)} %param.9), channel_id=1, source_target_pairs={{0,30},{2,0},{4,2},{6,4},{8,6},{10,8},{12,10},{14,12},{16,14},{18,... | collective-permute-start | bytes 9830408 | tf_op jit(solution)/shard_map/ppermute | solution.py:30
  49.4 32.0 %copy-start.6 = (bf16[2048,800]{0,1:T(8,128)(2,1)}, bf16[2048,800]{0,1:T(8,128)(2,1)S(1)}, u32[]{:S(2)}) copy-start(bf16[2048,800]{0,1:T(8,128)(2,1)S(1)} %collective-permute-done) | copy-start | bytes 9830404
  49.4 40.9 %collective-permute-start.2 = (bf16[2048,800]{0,1:T(8,128)(2,1)S(1)}, bf16[2048,800]{0,1:T(8,128)(2,1)S(1)}, u32[]{:S(2)}, u32[]{:S(2)}) collective-permute-start(bf16[2048,800]{0,1:T(8,128)(2,1)S(1)} %collective-permute-done), channel_id=1, source_target_pairs={{0,2},{2,4},{4,6},{6,8},{8,10},{10,12},{12,14},{14,16},{16,18},{18... | collective-permute-start | bytes 9830408 | tf_op jit(solution)/shard_map/ppermute | solution.py:27
  81.4 72.4 %copy-start.7 = (bf16[2048,800]{0,1:T(8,128)(2,1)}, bf16[2048,800]{0,1:T(8,128)(2,1)S(1)}, u32[]{:S(2)}) copy-start(bf16[2048,800]{0,1:T(8,128)(2,1)S(1)} %collective-permute-done.1) | copy-start | bytes 9830404
  81.4 72.4 %collective-permute-start.3 = (bf16[2048,800]{0,1:T(8,128)(2,1)S(1)}, bf16[2048,800]{0,1:T(8,128)(2,1)S(1)}, u32[]{:S(2)}, u32[]{:S(2)}) collective-permute-start(bf16[2048,800]{0,1:T(8,128)(2,1)S(1)} %collective-permute-done.1), channel_id=1, source_target_pairs={{0,30},{2,0},{4,2},{6,4},{8,6},{10,8},{12,10},{14,12},{16,14},{18,... | collective-permute-start | bytes 9830408 | tf_op jit(solution)/shard_map/ppermute | solution.py:30
  90.3 141.5 %copy-start.3 = (bf16[2048,800]{0,1:T(8,128)(2,1)}, bf16[2048,800]{0,1:T(8,128)(2,1)S(1)}, u32[]{:S(2)}) copy-start(bf16[2048,800]{0,1:T(8,128)(2,1)S(1)} %collective-permute-done.2) | copy-start | bytes 9830404
  90.3 69.0 %collective-permute-start.4 = (bf16[2048,800]{0,1:T(8,128)(2,1)S(1)}, bf16[2048,800]{0,1:T(8,128)(2,1)S(1)}, u32[]{:S(2)}, u32[]{:S(2)}) collective-permute-start(bf16[2048,800]{0,1:T(8,128)(2,1)S(1)} %collective-permute-done.2), channel_id=1, source_target_pairs={{0,2},{2,4},{4,6},{6,8},{8,10},{10,12},{12,14},{14,16},{16,18},{18... | collective-permute-start | bytes 9830408 | tf_op jit(solution)/shard_map/ppermute | solution.py:27
  153.8 72.4 %collective-permute-start.5 = (bf16[2048,800]{0,1:T(8,128)(2,1)S(1)}, bf16[2048,800]{0,1:T(8,128)(2,1)S(1)}, u32[]{:S(2)}, u32[]{:S(2)}) collective-permute-start(bf16[2048,800]{0,1:T(8,128)(2,1)S(1)} %collective-permute-done.3), channel_id=1, source_target_pairs={{0,30},{2,0},{4,2},{6,4},{8,6},{10,8},{12,10},{14,12},{16,14},{18,... | collective-permute-start | bytes 9830408 | tf_op jit(solution)/shard_map/ppermute | solution.py:30
  159.3 67.0 %copy-start.1 = (bf16[2048,800]{0,1:T(8,128)(2,1)}, bf16[2048,800]{0,1:T(8,128)(2,1)S(1)}, u32[]{:S(2)}) copy-start(bf16[2048,800]{0,1:T(8,128)(2,1)S(1)} %collective-permute-done.4) | copy-start | bytes 9830404
  159.3 72.4 %collective-permute-start.6 = (bf16[2048,800]{0,1:T(8,128)(2,1)S(1)}, bf16[2048,800]{0,1:T(8,128)(2,1)S(1)}, u32[]{:S(2)}, u32[]{:S(2)}) collective-permute-start(bf16[2048,800]{0,1:T(8,128)(2,1)S(1)} %collective-permute-done.4), channel_id=1, source_target_pairs={{0,2},{2,4},{4,6},{6,8},{8,10},{10,12},{12,14},{14,16},{16,18},{18... | collective-permute-start | bytes 9830408 | tf_op jit(solution)/shard_map/ppermute | solution.py:27
  226.3 72.5 %copy-start.4 = (bf16[2048,800]{0,1:T(8,128)(2,1)}, bf16[2048,800]{0,1:T(8,128)(2,1)S(1)}, u32[]{:S(2)}) copy-start(bf16[2048,800]{0,1:T(8,128)(2,1)S(1)} %collective-permute-done.5) | copy-start | bytes 9830404
  226.3 72.5 %collective-permute-start.7 = (bf16[2048,800]{0,1:T(8,128)(2,1)S(1)}, bf16[2048,800]{0,1:T(8,128)(2,1)S(1)}, u32[]{:S(2)}, u32[]{:S(2)}) collective-permute-start(bf16[2048,800]{0,1:T(8,128)(2,1)S(1)} %collective-permute-done.5), channel_id=1, source_target_pairs={{0,30},{2,0},{4,2},{6,4},{8,6},{10,8},{12,10},{14,12},{16,14},{18,... | collective-permute-start | bytes 9830408 | tf_op jit(solution)/shard_map/ppermute | solution.py:30
  231.8 67.0 %copy-start.8 = (bf16[2048,800]{0,1:T(8,128)(2,1)}, bf16[2048,800]{0,1:T(8,128)(2,1)S(1)}, u32[]{:S(2)}) copy-start(bf16[2048,800]{0,1:T(8,128)(2,1)S(1)} %collective-permute-done.6) | copy-start | bytes 9830404
  231.8 72.6 %collective-permute-start.8 = (bf16[2048,800]{0,1:T(8,128)(2,1)S(1)}, bf16[2048,800]{0,1:T(8,128)(2,1)}, u32[]{:S(2)}, u32[]{:S(2)}) collective-permute-start(bf16[2048,800]{0,1:T(8,128)(2,1)S(1)} %collective-permute-done.6), channel_id=1, source_target_pairs={{0,2},{2,4},{4,6},{6,8},{8,10},{10,12},{12,14},{14,16},{16,18},{18... | collective-permute-start | bytes 9830408 | tf_op jit(solution)/shard_map/ppermute | solution.py:27
  298.8 5.6 copy-start.10
  298.8 71.1 %collective-permute-start.9 = (bf16[2048,800]{0,1:T(8,128)(2,1)S(1)}, bf16[2048,800]{0,1:T(8,128)(2,1)}, u32[]{:S(2)}, u32[]{:S(2)}) collective-permute-start(bf16[2048,800]{0,1:T(8,128)(2,1)S(1)} %collective-permute-done.7), channel_id=1, source_target_pairs={{0,30},{2,0},{4,2},{6,4},{8,6},{10,8},{12,10},{14,12},{16,14},{18,... | collective-permute-start | bytes 9830408 | tf_op jit(solution)/shard_map/ppermute | solution.py:30
  304.4 71.4 %collective-permute-start.10 = (bf16[2048,800]{0,1:T(8,128)(2,1)}, bf16[2048,800]{0,1:T(8,128)(2,1)}, u32[]{:S(2)}, u32[]{:S(2)}) collective-permute-start(bf16[2048,800]{0,1:T(8,128)(2,1)} %collective-permute-done.8), channel_id=1, source_target_pairs={{0,2},{2,4},{4,6},{6,8},{8,10},{10,12},{12,14},{14,16},{16,18},{18... | collective-permute-start | bytes 9830408 | tf_op jit(solution)/shard_map/ppermute | solution.py:27
  369.9 104.6 %collective-permute-start.11 = (bf16[2048,800]{0,1:T(8,128)(2,1)}, bf16[2048,800]{0,1:T(8,128)(2,1)}, u32[]{:S(2)}, u32[]{:S(2)}) collective-permute-start(bf16[2048,800]{0,1:T(8,128)(2,1)} %collective-permute-done.9), channel_id=1, source_target_pairs={{0,30},{2,0},{4,2},{6,4},{8,6},{10,8},{12,10},{14,12},{16,14},{18,... | collective-permute-start | bytes 9830408 | tf_op jit(solution)/shard_map/ppermute | solution.py:30
  375.8 102.9 %collective-permute-start.12 = (bf16[2048,800]{0,1:T(8,128)(2,1)}, bf16[2048,800]{0,1:T(8,128)(2,1)}, u32[]{:S(2)}, u32[]{:S(2)}) collective-permute-start(bf16[2048,800]{0,1:T(8,128)(2,1)} %collective-permute-done.10), channel_id=1, source_target_pairs={{0,2},{2,4},{4,6},{6,8},{8,10},{10,12},{12,14},{14,16},{16,18},{18... | collective-permute-start | bytes 9830408 | tf_op jit(solution)/shard_map/ppermute | solution.py:27
  444.5 17.0 %copy-start = (bf16[2048,800]{0,1:T(8,128)(2,1)S(1)}, bf16[2048,800]{0,1:T(8,128)(2,1)}, u32[]{:S(2)}) copy-start(bf16[2048,800]{0,1:T(8,128)(2,1)} %param.9) | copy-start | bytes 9830404
  463.4 55.0 %copy-start.2 = (bf16[2048,800]{0,1:T(8,128)(2,1)S(1)}, bf16[2048,800]{0,1:T(8,128)(2,1)}, u32[]{:S(2)}) copy-start(bf16[2048,800]{0,1:T(8,128)(2,1)} %copy-done.1) | copy-start | bytes 9830404
  463.4 56.9 %copy-start.5 = (bf16[2048,800]{0,1:T(8,128)(2,1)S(1)}, bf16[2048,800]{0,1:T(8,128)(2,1)}, u32[]{:S(2)}) copy-start(bf16[2048,800]{0,1:T(8,128)(2,1)} %copy-done.4) | copy-start | bytes 9830404
  463.4 58.8 %copy-start.9 = (bf16[2048,800]{0,1:T(8,128)(2,1)S(1)}, bf16[2048,800]{0,1:T(8,128)(2,1)}, u32[]{:S(2)}) copy-start(bf16[2048,800]{0,1:T(8,128)(2,1)} %copy-done.8) | copy-start | bytes 9830404
  463.4 60.8 %copy-start.11 = (bf16[2048,800]{0,1:T(8,128)(2,1)S(1)}, bf16[2048,800]{0,1:T(8,128)(2,1)}, u32[]{:S(2)}) copy-start(bf16[2048,800]{0,1:T(8,128)(2,1)} %copy-done.10) | copy-start | bytes 9830404
  474.6 71.8 %collective-permute-start.13 = (bf16[2048,800]{0,1:T(8,128)(2,1)}, bf16[2048,800]{0,1:T(8,128)(2,1)S(1)}, u32[]{:S(2)}, u32[]{:S(2)}) collective-permute-start(bf16[2048,800]{0,1:T(8,128)(2,1)} %collective-permute-done.11), channel_id=1, source_target_pairs={{0,30},{2,0},{4,2},{6,4},{8,6},{10,8},{12,10},{14,12},{16,14},{18,... | collective-permute-start | bytes 9830408 | tf_op jit(solution)/shard_map/ppermute | solution.py:30
  478.6 69.7 %collective-permute-start.14 = (bf16[2048,800]{0,1:T(8,128)(2,1)}, bf16[2048,800]{0,1:T(8,128)(2,1)S(1)}, u32[]{:S(2)}, u32[]{:S(2)}) collective-permute-start(bf16[2048,800]{0,1:T(8,128)(2,1)} %collective-permute-done.12), channel_id=1, source_target_pairs={{0,2},{2,4},{4,6},{6,8},{8,10},{10,12},{12,14},{14,16},{16,18},{18... | collective-permute-start | bytes 9830408 | tf_op jit(solution)/shard_map/ppermute | solution.py:27
  524.2 26.1 %copy-start.12 = (bf16[512,2048]{1,0:T(8,128)(2,1)S(1)}, bf16[512,2048]{1,0:T(8,128)(2,1)}, u32[]{:S(2)}) copy-start(bf16[512,2048]{1,0:T(8,128)(2,1)} %all-gather.2.cloned.1.call-done) | copy-start | bytes 6291460
  550.3 40.1 %copy-start.13 = (s32[512]{0:T(512)S(1)}, s32[512]{0:T(512)}, u32[]{:S(2)}) copy-start(s32[512]{0:T(512)} %param.10) | copy-start | bytes 6148
  585.3 23.7 %copy-start.16 = (s32[512]{0:T(512)S(1)}, s32[512]{0:T(512)}, u32[]{:S(2)}) copy-start(s32[512]{0:T(512)} %param.11) | copy-start | bytes 6148
  585.3 23.7 %copy-start.17 = (s32[16]{0:T(128)S(1)}, s32[16]{0:T(128)}, u32[]{:S(2)}) copy-start(s32[16]{0:T(128)} %param.13) | copy-start | bytes 196
  609.0 52.1 %copy-start.14 = (f32[256]{0:T(256)}, f32[256]{0:T(256)S(1)}, u32[]{:S(2)}) copy-start(f32[256]{0:T(256)S(1)} %get-tuple-element.13) | copy-start | bytes 3076
  609.6 51.5 %copy-start.15 = (f32[256]{0:T(256)}, f32[256]{0:T(256)S(1)}, u32[]{:S(2)}) copy-start(f32[256]{0:T(256)S(1)} %subtract_multiply_fusion.1) | copy-start | bytes 3076
Sparse Core Ops, SparseCore 0:
  370.1 69.9 all-gather.1
